TPU v7x, 256 devices: a whole 4x4x8 slice. The times are simulated.
256 devices in a mesh: dp: 8 (over y, core), mp: 32 (over z, x).
Axes of the slice: x: 4, y: 4, z: 8, core: 2. Of those that a mesh axis runs over, the one named last changes fastest.
Arguments:
- table: bfloat16 [32, 2048, 128], P('mp'), may hold values from -6 to 6
- ids: int32 [65536, 32, 2], P('dp', 'mp'), may hold values from 0 to 2047
- counts: int32 [256, 8], P(('dp', 'mp')), may hold values from 1 to 96, 256 in all within a row
- labels: int32 [65536], P(('dp', 'mp')), may hold values from 0 to 4
- request_home: int32 [2048], replicated, may hold values from 0 to 2047, each once
- user_codes: bfloat16 [2048, 1024], P('dp'), may hold values from -6 to 6
- cross_down: bfloat16 [4096, 256], replicated, may hold values from -0.09375 to 0.09375
- cross_up: bfloat16 [256, 4096], replicated, may hold values from -0.375 to 0.375
- cross_bias: float32 [4096], replicated, may hold values from -4 to 4
- tower_weight: bfloat16 [4096, 1024], P('mp'), may hold values from -0.09375 to 0.09375
- tower_bias: float32 [1024], replicated, may hold values from -3 to 3
Outputs:
- scores: float32 [65536], P(('dp', 'mp'))
- pooled_grad: bfloat16 [65536, 32, 128], P('dp', 'mp')
Inputs may be any that keep to these rules, and one draw needn't show every extreme that they name: `counts`: each row sums to 256; its largest entry is exactly 96. `request_home`: a permutation of the request slots.
All inputs are finite; a program needn't handle non-finite values.
Results may differ from a plain program's by a relative error of at most 0.0097.
Values may be sent and summed in bfloat16 or wider, within the bound.
No kernel may reach another device: no remote copies, remote signals or barrier semaphores. Data moves between devices by JAX's collectives and lax.ppermute only.
A program may use at most 128 MiB of HBM per device.

v0:
```python
import jax
import jax.numpy as jnp
from jax import lax
from jax.sharding import PartitionSpec as P


def members(counts_row, rows):
    ends = jnp.cumsum(counts_row)
    starts = ends - counts_row
    place = jnp.arange(rows, dtype=jnp.int32)[:, None]
    return (place >= starts[None, :]) & (place < ends[None, :])


def dot_last(left, right):
    return lax.dot_general(
        left, right, (((1,), (1,)), ((), ())), preferred_element_type=jnp.float32
    )


def pair_grad(scores, member, labels):
    gain = jnp.exp2(labels.astype(jnp.float32))
    member_f = member.astype(jnp.float32)
    same = jnp.dot(member_f, member_f.T) > 0.5
    diff = gain[:, None] - gain[None, :]
    gap = scores[None, :] - scores[:, None]
    turn = jnp.where(diff > 0, jax.nn.sigmoid(gap), jax.nn.sigmoid(-gap))
    total = jnp.sum(jnp.where(same, diff * turn, 0.0), axis=1)
    seg_gain = jnp.sum(jnp.where(member, (gain - 1.0)[:, None], 0.0), axis=0)
    norm = jnp.sum(jnp.where(member, seg_gain[None, :], 0.0), axis=1)
    return -total / jnp.maximum(norm, 1.0)


def local(
    table,
    ids,
    counts,
    labels,
    request_home,
    user_codes,
    cross_down,
    cross_up,
    cross_bias,
    tower_weight,
    tower_bias,
):
    f32, bf16 = (jnp.float32, jnp.bfloat16)
    n_mp = lax.axis_size("mp")
    n_dp = lax.axis_size("dp")
    d_idx = lax.axis_index("dp")
    m_idx = lax.axis_index("mp")
    rows = labels.shape[0]
    seg_count = counts.shape[1]
    width = user_codes.shape[1]
    emb = table.shape[2]
    rank = cross_down.shape[1]
    scale = 1.0 / jnp.sqrt(jnp.float32(width))
    piece = tower_weight.shape[1] // n_dp
    w_piece = lax.dynamic_slice_in_dim(tower_weight, d_idx * piece, piece, axis=1)
    w_cols = lax.all_gather(w_piece, "mp", axis=0, tiled=True)
    w_all = lax.all_gather(w_cols, "dp", axis=1, tiled=True)
    w3 = w_all.reshape(n_mp, emb, width)
    held = user_codes.shape[0]
    home_local = lax.dynamic_slice_in_dim(request_home, d_idx * held, held)
    wanted = (
        (jnp.arange(n_dp, dtype=jnp.int32)[:, None] * n_mp + m_idx) * seg_count
        + jnp.arange(seg_count, dtype=jnp.int32)[None, :]
    ).reshape(-1)
    pick = (home_local[None, :] == wanted[:, None]).astype(bf16)
    mine = jnp.dot(pick, user_codes, preferred_element_type=f32).astype(bf16)
    user_seg = lax.psum_scatter(
        mine.reshape(n_dp, seg_count, width), "dp", scatter_dimension=0, tiled=False
    )
    slab = table[0]
    picked = jnp.take(slab, ids[:, 0, :], axis=0, mode="clip")
    pooled = jnp.sum(picked.astype(f32), axis=1).astype(bf16)
    x0f = lax.all_to_all(
        pooled.reshape(n_mp, rows, emb), "mp", split_axis=0, concat_axis=0, tiled=True
    )
    member = members(counts[0], rows)
    cd3 = cross_down.reshape(n_mp, emb, rank)
    cu3 = cross_up.reshape(rank, n_mp, emb)
    bias3 = cross_bias.reshape(n_mp, 1, emb)
    z = jnp.einsum("fcd,fdr->cr", x0f, cd3, preferred_element_type=f32).astype(bf16)
    cross = jnp.einsum("cr,rfd->fcd", z, cu3, preferred_element_type=f32) + bias3
    x1 = (x0f * cross + x0f).astype(bf16)
    act = jnp.einsum("fcd,fdh->ch", x1, w3, preferred_element_type=f32) + tower_bias
    sig = jax.nn.sigmoid(act)
    hidden = (act * sig).astype(bf16)
    pair = dot_last(hidden, user_seg)
    score = jnp.sum(jnp.where(member, pair, 0.0), axis=1) * scale
    dscore = pair_grad(score, member, labels)
    code = jnp.dot(member.astype(bf16), user_seg, preferred_element_type=f32)
    slope = sig * (1.0 + act * (1.0 - sig))
    dact = (dscore[:, None] * code * scale * slope).astype(bf16)
    dx1 = jnp.einsum("ch,fdh->fcd", dact, w3, preferred_element_type=f32)
    dcross = (dx1 * x0f).astype(bf16)
    dz = jnp.einsum("fcd,rfd->cr", dcross, cu3, preferred_element_type=f32).astype(bf16)
    dx0 = dx1 * (1.0 + cross) + jnp.einsum("cr,fdr->fcd", dz, cd3, preferred_element_type=f32)
    grads = dx0.astype(bf16)
    returned = lax.all_to_all(grads, "mp", split_axis=0, concat_axis=0, tiled=True)
    return (score, returned.reshape(n_mp * rows, 1, emb))


def solution(mesh):
    in_specs = (
        P("mp", None, None),
        P("dp", "mp", None),
        P(("dp", "mp"), None),
        P(("dp", "mp")),
        P(),
        P("dp", None),
        P(),
        P(),
        P(),
        P("mp", None),
        P(),
    )
    out_specs = (P(("dp", "mp")), P("dp", "mp", None))
    return jax.shard_map(local, mesh=mesh, in_specs=in_specs, out_specs=out_specs, check_vma=False)
```

profile of v0, /device:TPU:10, one launch (start us, length us, event | category | flops | bytes accessed | tf_op | source)
XLA Modules:
  0.0 346.3 jit_solution(14947742715400940034)
XLA Ops:
  7.2 0.0 copy-start
  7.2 0.0 all-gather.3.cloned.1.call-start
  7.2 1.5 constant_dynamic-slice_fusion
  8.7 0.0 all-gather.3.cloned.1.call-update
  8.8 0.0 all-gather.5.cloned.1.call-start
  8.8 80.5 %all-gather.3.cloned.1.call-done = bf16[4096,128]{1,0:T(8,128)(2,1)} async-done(((bf16[128,128]{1,0:T(8,128)(2,1)}), bf16[4096,128]{1,0:T(8,128)(2,1)}) %all-gather.3.cloned.1.call-update) | async-done | bytes 1048592 | tf_op jit(solution)/shard_map/all_gather | solution.py:59
  89.3 0.0 all-gather.5.cloned.1.call-update
  89.3 3.4 copy.18
  92.7 0.0 copy-start.1
  92.7 4.1 %reshape.87 = s32[16384]{0:T(1024)S(1)} reshape(s32[8192,1,2]{2,0,1:T(8,128)} %copy.18) | data formatting | bytes 131072 | tf_op jit(solution)/shard_map/jit(_take)/broadcast_in_dim | solution.py:74
  96.8 0.0 copy-done.1
  96.8 57.8 %gather_fusion = bf16[16384,128]{1,0:T(8,128)(2,1)} fusion(bf16[2048,128]{1,0:T(8,128)(2,1)S(1)} %bitcast.114, s32[16384]{0:T(1024)S(1)} %broadcast_clamp_fusion), kind=kCustom, calls=%fused_computation | custom fusion | bytes 8454144 | tf_op jit(solution)/shard_map/jit(_take)/gather | solution.py:74
  154.6 45.8 %reduce_sum.48 = bf16[8192,128]{1,0:T(8,128)(2,1)} reduce(bf16[8192,2,128]{2,1,0:T(2,128)(2,1)} %bitcast.115, bf16[]{:T(256)} %constant.18.clone.1), dimensions={1}, to_apply=%region_1.2 | reduce | flops 1048576 | bytes 6291458 | tf_op jit(solution)/shard_map/reduce_sum | solution.py:75
  200.4 0.0 copy-start.2
  200.5 0.0 copy-start.8
  200.5 0.0 copy-start.4
  200.5 7.7 %all-to-all-start = ((bf16[32,256,128]{2,1,0:T(8,128)(2,1)}), bf16[32,256,128]{2,1,0:T(8,128)(2,1)}, u32[]{:S(2)}, u32[]{:S(2)}) async-start(bf16[32,256,128]{2,1,0:T(8,128)(2,1)} %bitcast.116), calls=%async_computation | async-start | bytes 4194304 | tf_op jit(solution)/shard_map/all_to_all | solution.py:76
  208.1 0.2 reduce-scatter.2.cloned.1.call-start
  208.4 0.1 iota_add_fusion
  208.4 0.1 add.100
  208.5 0.8 dynamic_slice.7
  209.3 0.0 copy-done.2
  209.3 0.9 fusion.36
  210.2 0.0 reduce-scatter.2.cloned.1.call-update
  210.2 0.0 copy-done.8
  210.2 0.2 reduce-window.4
  210.4 0.0 copy-done.4
  210.4 0.2 select_reduce_fusion.1
  210.6 0.1 select_reduce_fusion
  210.7 42.6 %all-to-all-done = bf16[32,256,128]{2,1,0:T(8,128)(2,1)} async-done(((bf16[32,256,128]{2,1,0:T(8,128)(2,1)}), bf16[32,256,128]{2,1,0:T(8,128)(2,1)}, u32[]{:S(2)}, u32[]{:S(2)}) %all-to-all-start) | async-done | bytes 2097184 | tf_op jit(solution)/shard_map/all_to_all | solution.py:76
  253.3 0.0 copy-done
  253.3 0.0 copy-start.3
  253.3 0.0 copy-start.7
  253.3 6.6 %fusion.8 = f32[256,32,128]{2,0,1:T(8,128)} fusion(bf16[32,256,128]{2,1,0:T(8,128)(2,1)} %all-to-all-done, bf16[32,128,256]{2,1,0:T(8,128)(2,1)S(1)} %bitcast.112, bf16[256,4096]{1,0:T(8,128)(2,1)} %param.18), kind=kOutput, calls=%fused_computation.12 | convolution fusion | flops 1073807360 | bytes 10485760 | tf_op jit(solution)/shard_map/cr,rfd->fcd/dot_general | solution.py:84
  259.9 0.0 copy-done.3
  259.9 0.0 copy-done.7
  259.9 6.7 %fusion.18 = f32[256,1024]{1,0:T(8,128)S(1)} fusion(bf16[32,128,1024]{2,1,0:T(8,128)(2,1)} %bitcast.125, bf16[32,256,128]{2,1,0:T(8,128)(2,1)} %all-to-all-done, f32[256,32,128]{2,0,1:T(8,128)} %fusion.8, f32[32,128]{1,0:T(8,128)S(1)} %bitcast.118, f32[1024]{0:T(1024)S(1)} %copy-done.7), kind=kOutput, calls=%fused_computation.21 | convolution fusion | flops 2152988672 | bytes 15749120 | tf_op jit(solution)/shard_map/fcd,fdh->ch/dot_general | solution.py:86
  266.6 0.0 reduce-scatter.2.cloned.1.call-done
  266.6 1.1 fusion.47
  267.8 0.0 copy-start.6
  267.8 0.0 copy-start.5
  267.8 0.4 fusion.35
  268.2 0.3 copy-done.6
  268.5 7.1 %fusion.48 = f32[32,128,256]{1,2,0:T(8,128)} fusion(bf16[32,128,1024]{2,1,0:T(8,128)(2,1)} %bitcast.126, f32[256,1024]{1,0:T(8,128)S(1)} %fusion.18, f32[256]{0:T(256)S(1)} %maximum_divide_fusion, bf16[1,8,1024]{2,1,0:T(8,128)(2,1)S(1)} %copy-done.6, s32[8]{0:T(128)S(1)} %bitcast.124, s32[8]{0:T(128)S(1)} %fusion.65), kind=kOutput, calls=%fused_computation.39 | convolution fusion | flops 2154567680 | bytes 13648960 | tf_op jit(solution)/shard_map/ch,fdh->fcd/dot_general | solution.py:95
  275.6 0.0 copy-done.5
  275.6 9.6 %fusion.2 = bf16[32,256,128]{2,1,0:T(8,128)(2,1)} fusion(f32[32,128,256]{1,2,0:T(8,128)} %fusion.48, f32[256,32,128]{2,0,1:T(8,128)} %fusion.8, bf16[32,128,256]{2,1,0:T(8,128)(2,1)S(1)} %bitcast.113, f32[32,128]{1,0:T(8,128)S(1)} %bitcast.119, bf16[32,256,128]{2,1,0:T(8,128)(2,1)} %all-to-all-done, bf16[256,4096]{1,0:T(8,128)(2,1)} %param.18), kind=kOutput, calls=%fused_computation.6 | convolution fusion | flops 1082195968 | bytes 16793600 | tf_op jit(solution)/shard_map/cr,fdr->fcd/dot_general | solution.py:98
  285.2 53.3 %all_to_all.10 = bf16[32,256,128]{2,1,0:T(8,128)(2,1)S(1)} all-to-all(bf16[32,256,128]{2,1,0:T(8,128)(2,1)} %fusion.2), channel_id=1, replica_groups=mesh['dp'=8,'mp'=32] {'mp'}, dimensions={0} | all-to-all | bytes 4194304 | tf_op jit(solution)/shard_map/all_to_all | solution.py:100
  338.4 1.3 copy.43
  (7 shorter events, 0.0 us)
Async XLA Ops:
  7.2 246.1 %copy-start = (bf16[4096,256]{1,0:T(8,128)(2,1)S(1)}, bf16[4096,256]{1,0:T(8,128)(2,1)}, u32[]{:S(2)}) copy-start(bf16[4096,256]{1,0:T(8,128)(2,1)} %param.17) | copy-start | bytes 6291460
  7.2 82.1 %all-gather.3.cloned.1.call-start = ((), (), s32[]{:S(2)}) async-start(), calls=%async_computation.3 | async-start | bytes 1081344 | tf_op jit(solution)/shard_map/all_gather | solution.py:59
  8.8 251.1 %all-gather.5.cloned.1.call-start = ((), (), s32[]{:S(2)}) async-start(), calls=%async_computation.4 | async-start | bytes 9437184 | tf_op jit(solution)/shard_map/all_gather | solution.py:60
  92.7 4.1 %copy-start.1 = (bf16[1,2048,128]{2,1,0:T(8,128)(2,1)S(1)}, bf16[1,2048,128]{2,1,0:T(8,128)(2,1)}, u32[]{:S(2)}) copy-start(bf16[1,2048,128]{2,1,0:T(8,128)(2,1)} %param.11) | copy-start | bytes 1572868
  200.4 8.8 %copy-start.2 = (bf16[256,1024]{1,0:T(8,128)(2,1)S(1)}, bf16[256,1024]{1,0:T(8,128)(2,1)}, u32[]{:S(2)}) copy-start(bf16[256,1024]{1,0:T(8,128)(2,1)} %param.16) | copy-start | bytes 1572868
  200.5 9.8 %copy-start.8 = (s32[1,8]{1,0:T(1,128)S(1)}, s32[1,8]{1,0:T(1,128)}, u32[]{:S(2)}) copy-start(s32[1,8]{1,0:T(1,128)} %param.13) | copy-start | bytes 100
  200.5 10.0 %copy-start.4 = (s32[256]{0:T(256)S(1)}, s32[256]{0:T(256)}, u32[]{:S(2)}) copy-start(s32[256]{0:T(256)} %param.14) | copy-start | bytes 3076
  200.5 52.8 %all-to-all-start = ((bf16[32,256,128]{2,1,0:T(8,128)(2,1)}), bf16[32,256,128]{2,1,0:T(8,128)(2,1)}, u32[]{:S(2)}, u32[]{:S(2)}) async-start(bf16[32,256,128]{2,1,0:T(8,128)(2,1)} %bitcast.116), calls=%async_computation | async-start | bytes 4194304 | tf_op jit(solution)/shard_map/all_to_all | solution.py:76
  208.1 58.5 %reduce-scatter.2.cloned.1.call-start = ((), (), s32[]{:S(2)}) async-start(), calls=%async_computation.5 | async-start | bytes 147456 | tf_op jit(solution)/shard_map/reduce_scatter | solution.py:70
  253.3 6.6 %copy-start.3 = (f32[4096]{0:T(1024)S(1)}, f32[4096]{0:T(1024)}, u32[]{:S(2)}) copy-start(f32[4096]{0:T(1024)} %param.19) | copy-start | bytes 49156
  253.3 6.6 %copy-start.7 = (f32[1024]{0:T(1024)S(1)}, f32[1024]{0:T(1024)}, u32[]{:S(2)}) copy-start(f32[1024]{0:T(1024)} %param.21) | copy-start | bytes 12292
  267.8 0.7 copy-start.6
  267.8 7.8 %copy-start.5 = (f32[256]{0:T(256)}, f32[256]{0:T(256)S(1)}, u32[]{:S(2)}) copy-start(f32[256]{0:T(256)S(1)} %broadcast_multiply_fusion) | copy-start | bytes 3076
Sparse Core Ops, SparseCore 0:
  11.1 78.0 all-gather.2
  91.1 54.5 all-gather.4
  211.4 31.8 reduce-scatter.1
where the time goes:
time: 347 us; the launch traced here: 346 us
  waiting for transfers between devices  123 us (35%)
  local copies, waits for them, and re-layouts  69.3 us (20%)
  blocking collectives  53.3 us (15%)
  other arithmetic  46.4 us (13%)
  matrix products  32.4 us (9%)
  between operations  13.9 us (4%)
  starting transfers between devices  7.95 us (2%)
    all_gather x1, waiting for transfers between devices, local(): w_cols = lax.all_gather(w_piece, 'mp', axis=0, tiled=True)  80.5 us
    gather x1, local copies, waits for them, and re-layouts, local(): picked = jnp.take(slab, ids[:, 0, :], axis=0, mode='clip')  57.8 us
    all_to_all x1, blocking collectives, local(): lax.all_to_all(grads, 'mp', split_axis=0, concat_axis=0, tiled=True)  53.3 us
    reduce_sum x1, other arithmetic, local(): pooled = jnp.sum(picked.astype(f32), axis=1).astype(bf16)  45.8 us
    all_to_all x1, waiting for transfers between devices, local(): lax.all_to_all(pooled.reshape(n_mp, rows, emb), 'mp', split_axis=0, conca...  42.6 us
    dot_general x1, matrix products, local(): jnp.einsum('cr,fdr->fcd', dz, cd3, preferred_element_type=f32)  9.56 us
    all_to_all x1, starting transfers between devices, local(): lax.all_to_all(pooled.reshape(n_mp, rows, emb), 'mp', split_axis=0, conca...  7.65 us
    dot_general x1, matrix products, local(): dx1 = jnp.einsum('ch,fdh->fcd', dact, w3, preferred_element_type=f32)  7.13 us
  transfers between devices with their start and end apart: 4, of which 2 were waited for; matrix products, arithmetic and copies ran while one was open for 37% of the time, Pallas kernels for 0%

commit v1 on v0

--- a/solution.py
+++ b/solution.py
@@ -1,7 +1,18 @@
+import functools
 import jax
 import jax.numpy as jnp
 from jax import lax
 from jax.sharding import PartitionSpec as P
+
+
+def place_ticks_now(block_here, across):
+    last = tuple((block_here for _ in range(lax.axis_size(across))))
+    mat_out = jnp.stack(last, axis=0)
+    arr_now = lax.all_to_all(mat_out, across, 0, 0)
+    return jnp.concatenate(arr_now, axis=1)
+
+
+write_trails = functools.partial(place_ticks_now, across="dp")
 
 
 def members(counts_row, rows):
@@ -57,7 +68,7 @@
     piece = tower_weight.shape[1] // n_dp
     w_piece = lax.dynamic_slice_in_dim(tower_weight, d_idx * piece, piece, axis=1)
     w_cols = lax.all_gather(w_piece, "mp", axis=0, tiled=True)
-    w_all = lax.all_gather(w_cols, "dp", axis=1, tiled=True)
+    w_all = write_trails(w_cols)
     w3 = w_all.reshape(n_mp, emb, width)
     held = user_codes.shape[0]
     home_local = lax.dynamic_slice_in_dim(request_home, d_idx * held, held)

time: 347 us -> 434 us (1.25)
  waiting for transfers between devices: 123 us -> 165 us
  local copies, waits for them, and re-layouts: 69.3 us -> 97.7 us
  starting transfers between devices: 7.95 us -> 17.2 us
  blocking collectives: 53.3 us -> 57.7 us
    all_to_all x0 -> x1, waiting for transfers between devices: none -> 85 us  [place_ticks_now(): arr_now = lax.all_to_all(mat_out, across, 0, 0)]
    all_to_all x1, waiting for transfers between devices: 42.6 us -> 0.01 us  [local(): lax.all_to_all(pooled.reshape(n_mp, rows, emb), 'mp', split_axis=0, conca...]
    another operation x0 -> x2, local copies, waits for them, and re-layouts: none -> 18.8 us  [the longest x1 13.3 us: local(): w3 = w_all.reshape(n_mp, emb, width)]
    reshape x0 -> x1, local copies, waits for them, and re-layouts: none -> 10.3 us  [place_ticks_now(): return jnp.concatenate(arr_now, axis=1)]
    all_to_all x0 -> x1, starting transfers between devices: none -> 5.51 us  [place_ticks_now(): arr_now = lax.all_to_all(mat_out, across, 0, 0)]
    all_to_all x1, blocking collectives: 53.3 us -> 57.7 us  [local(): lax.all_to_all(grads, 'mp', split_axis=0, concat_axis=0, tiled=True)]
  transfers between devices with their start and end apart: 4 -> 4, of which waited for: 2 -> 2; matrix products, arithmetic and copies ran while one was open for 37% -> 9% of each run, Pallas kernels for 0% -> 0%
where the time goes in v1:
time: 434 us; the launch traced here: 432 us
  waiting for transfers between devices  165 us (38%)
  local copies, waits for them, and re-layouts  97.7 us (23%)
  blocking collectives  57.7 us (13%)
  other arithmetic  46.4 us (11%)
  matrix products  32.5 us (7%)
  starting transfers between devices  17.2 us (4%)
  between operations  15.6 us (4%)
    all_to_all x1, waiting for transfers between devices, place_ticks_now(): arr_now = lax.all_to_all(mat_out, across, 0, 0)  85 us
    all_gather x1, waiting for transfers between devices, local(): w_cols = lax.all_gather(w_piece, 'mp', axis=0, tiled=True)  79.9 us
    all_to_all x1, blocking collectives, local(): lax.all_to_all(grads, 'mp', split_axis=0, concat_axis=0, tiled=True)  57.7 us
    gather x1, local copies, waits for them, and re-layouts, local(): picked = jnp.take(slab, ids[:, 0, :], axis=0, mode='clip')  57.4 us
    reduce_sum x1, other arithmetic, local(): pooled = jnp.sum(picked.astype(f32), axis=1).astype(bf16)  45.8 us
    another operation x1, local copies, waits for them, and re-layouts, local(): w3 = w_all.reshape(n_mp, emb, width)  13.3 us
    all_to_all x1, starting transfers between devices, local(): lax.all_to_all(pooled.reshape(n_mp, rows, emb), 'mp', split_axis=0, conca...  11.7 us
    reshape x1, local copies, waits for them, and re-layouts, place_ticks_now(): return jnp.concatenate(arr_now, axis=1)  10.3 us
  transfers between devices with their start and end apart: 4, of which 2 were waited for; matrix products, arithmetic and copies ran while one was open for 9% of the time, Pallas kernels for 0%

profile of v1, /device:TPU:10, one launch (start us, length us, event | category | flops | bytes accessed | tf_op | source)
XLA Modules:
  0.0 432.0 jit_solution(4329525168744055136)
XLA Ops:
  8.0 0.0 copy-start
  8.0 0.0 copy-start.1
  8.0 3.5 copy.18
  11.5 4.0 reshape.89
  15.6 0.0 copy-done.1
  15.6 57.4 %gather_fusion = bf16[16384,128]{1,0:T(8,128)(2,1)} fusion(bf16[2048,128]{1,0:T(8,128)(2,1)S(1)} %bitcast.114, s32[16384]{0:T(1024)S(1)} %broadcast_clamp_fusion), kind=kCustom, calls=%fused_computation | custom fusion | bytes 8454144 | tf_op jit(solution)/shard_map/jit(_take)/gather | solution.py:85
  73.0 45.8 %reduce_sum.48 = bf16[8192,128]{1,0:T(8,128)(2,1)} reduce(bf16[8192,2,128]{2,1,0:T(2,128)(2,1)} %bitcast.115, bf16[]{:T(256)} %constant.18.clone.1), dimensions={1}, to_apply=%region_1.2 | reduce | flops 1048576 | bytes 6291458 | tf_op jit(solution)/shard_map/reduce_sum | solution.py:86
  118.8 11.7 %all-to-all-start = ((bf16[32,256,128]{2,1,0:T(8,128)(2,1)}), bf16[32,256,128]{2,1,0:T(8,128)(2,1)}, u32[]{:S(2)}, u32[]{:S(2)}) async-start(bf16[32,256,128]{2,1,0:T(8,128)(2,1)} %bitcast.116), calls=%async_computation | async-start | bytes 4194304 | tf_op jit(solution)/shard_map/all_to_all | solution.py:87
  130.5 0.0 all-gather.2.cloned.1.call-start
  130.5 1.4 constant_dynamic-slice_fusion
  131.9 0.0 all-gather.2.cloned.1.call-update
  131.9 79.9 %all-gather.2.cloned.1.call-done = bf16[4096,128]{1,0:T(8,128)(2,1)} async-done(((bf16[128,128]{1,0:T(8,128)(2,1)}), bf16[4096,128]{1,0:T(8,128)(2,1)}) %all-gather.2.cloned.1.call-update) | async-done | bytes 1048592 | tf_op jit(solution)/shard_map/all_gather | solution.py:70
  211.8 0.0 all-to-all-done
  211.8 5.5 %stack.2 = bf16[8,4096,128]{2,1,0:T(8,128)(2,1)} broadcast(bf16[4096,128]{1,0:T(8,128)(2,1)} %all-gather.2.cloned.1.call-done), dimensions={1,2} | broadcast | bytes 9437184 | tf_op jit(solution)/shard_map/stack | solution.py:10
  217.3 0.0 copy-start.2
  217.3 0.0 copy-start.8
  217.3 5.5 %all-to-all-start.1 = ((bf16[8,4096,128]{2,1,0:T(8,128)(2,1)}), bf16[8,4096,128]{2,1,0:T(8,128)(2,1)}, u32[]{:S(2)}, u32[]{:S(2)}) async-start(bf16[8,4096,128]{2,1,0:T(8,128)(2,1)} %stack.2), calls=%async_computation.1 | async-start | bytes 16777216 | tf_op jit(solution)/shard_map/all_to_all | solution.py:11
  222.8 0.0 reduce-scatter.2.cloned.1.call-start
  222.8 0.1 iota_add_fusion
  222.9 0.1 add.100
  223.0 0.8 dynamic_slice.7
  223.8 0.0 copy-done.2
  223.8 0.9 fusion.36
  224.7 0.0 reduce-scatter.2.cloned.1.call-update
  224.7 0.0 copy-done.8
  224.7 0.2 reduce-window.4
  224.9 0.0 copy-done.4
  224.9 0.2 select_reduce_fusion.1
  225.1 0.1 select_reduce_fusion
  225.2 0.0 copy-done
  225.2 6.5 %fusion.8 = f32[256,32,128]{2,0,1:T(8,128)} fusion(bf16[32,256,128]{2,1,0:T(8,128)(2,1)} %all-to-all-done, bf16[32,128,256]{2,1,0:T(8,128)(2,1)S(1)} %bitcast.112, bf16[256,4096]{1,0:T(8,128)(2,1)} %param.18), kind=kOutput, calls=%fused_computation.12 | convolution fusion | flops 1073807360 | bytes 10485760 | tf_op jit(solution)/shard_map/cr,rfd->fcd/dot_general | solution.py:95
  231.7 85.0 %all-to-all-done.1 = bf16[8,4096,128]{2,1,0:T(8,128)(2,1)} async-done(((bf16[8,4096,128]{2,1,0:T(8,128)(2,1)}), bf16[8,4096,128]{2,1,0:T(8,128)(2,1)}, u32[]{:S(2)}, u32[]{:S(2)}) %all-to-all-start.1) | async-done | bytes 8388640 | tf_op jit(solution)/shard_map/all_to_all | solution.py:11
  316.7 10.3 %copy.20 = bf16[4096,8,128]{2,1,0:T(8,128)(2,1)} copy(bf16[4096,8,128]{2,0,1:T(8,128)(2,1)} %bitcast.12) | data formatting | bytes 16777216 | tf_op jit(solution)/shard_map/reshape | solution.py:12
  327.0 13.3 %reshape_reshape.3 = bf16[32,128,1024]{2,1,0:T(8,128)(2,1)} reshape(bf16[4096,8,128]{2,1,0:T(8,128)(2,1)} %copy.20) | data formatting | bytes 16777216 | tf_op jit(solution)/shard_map/reshape;reshape | solution.py:72
  340.4 0.0 copy-done.3
  340.4 0.0 copy-done.7
  340.4 6.7 %fusion.18 = f32[256,1024]{1,0:T(8,128)S(1)} fusion(bf16[32,128,1024]{2,1,0:T(8,128)(2,1)} %reshape_reshape.3, bf16[32,256,128]{2,1,0:T(8,128)(2,1)} %all-to-all-done, f32[256,32,128]{2,0,1:T(8,128)} %fusion.8, f32[32,128]{1,0:T(8,128)S(1)} %bitcast.118, f32[1024]{0:T(1024)S(1)} %copy-done.7), kind=kOutput, calls=%fused_computation.21 | convolution fusion | flops 2152988672 | bytes 15749120 | tf_op jit(solution)/shard_map/fcd,fdh->ch/dot_general | solution.py:97
  347.1 0.0 reduce-scatter.2.cloned.1.call-done
  347.1 0.0 copy-start.6
  347.1 1.2 fusion.47
  348.3 0.0 copy-start.5
  348.3 0.4 fusion.35
  348.7 0.0 copy-done.6
  348.7 7.1 %fusion.48 = f32[32,128,256]{1,2,0:T(8,128)} fusion(bf16[32,128,1024]{2,1,0:T(8,128)(2,1)} %reshape_reshape.3, f32[256,1024]{1,0:T(8,128)S(1)} %fusion.18, f32[256]{0:T(256)S(1)} %maximum_divide_fusion, bf16[1,8,1024]{2,1,0:T(8,128)(2,1)S(1)} %copy-done.6, s32[8]{0:T(128)S(1)} %bitcast.124, s32[8]{0:T(128)S(1)} %fusion.65), kind=kOutput, calls=%fused_computation.39 | convolution fusion | flops 2154567680 | bytes 13648960 | tf_op jit(solution)/shard_map/ch,fdh->fcd/dot_general | solution.py:106
  355.8 0.0 copy-done.5
  355.8 9.7 %fusion.2 = bf16[32,256,128]{2,1,0:T(8,128)(2,1)} fusion(f32[32,128,256]{1,2,0:T(8,128)} %fusion.48, f32[256,32,128]{2,0,1:T(8,128)} %fusion.8, bf16[32,128,256]{2,1,0:T(8,128)(2,1)S(1)} %bitcast.113, f32[32,128]{1,0:T(8,128)S(1)} %bitcast.119, bf16[32,256,128]{2,1,0:T(8,128)(2,1)} %all-to-all-done, bf16[256,4096]{1,0:T(8,128)(2,1)} %param.18), kind=kOutput, calls=%fused_computation.6 | convolution fusion | flops 1082195968 | bytes 16793600 | tf_op jit(solution)/shard_map/cr,fdr->fcd/dot_general | solution.py:109
  365.5 57.7 %all_to_all.15 = bf16[32,256,128]{2,1,0:T(8,128)(2,1)S(1)} all-to-all(bf16[32,256,128]{2,1,0:T(8,128)(2,1)} %fusion.2), channel_id=1, replica_groups=mesh['dp'=8,'mp'=32] {'mp'}, dimensions={0} | all-to-all | bytes 4194304 | tf_op jit(solution)/shard_map/all_to_all | solution.py:111
  423.3 1.3 copy.42
  (9 shorter events, 0.0 us)
Async XLA Ops:
  8.0 217.2 %copy-start = (bf16[4096,256]{1,0:T(8,128)(2,1)S(1)}, bf16[4096,256]{1,0:T(8,128)(2,1)}, u32[]{:S(2)}) copy-start(bf16[4096,256]{1,0:T(8,128)(2,1)} %param.17) | copy-start | bytes 6291460
  8.0 7.6 %copy-start.1 = (bf16[1,2048,128]{2,1,0:T(8,128)(2,1)S(1)}, bf16[1,2048,128]{2,1,0:T(8,128)(2,1)}, u32[]{:S(2)}) copy-start(bf16[1,2048,128]{2,1,0:T(8,128)(2,1)} %param.11) | copy-start | bytes 1572868
  118.8 93.0 %all-to-all-start = ((bf16[32,256,128]{2,1,0:T(8,128)(2,1)}), bf16[32,256,128]{2,1,0:T(8,128)(2,1)}, u32[]{:S(2)}, u32[]{:S(2)}) async-start(bf16[32,256,128]{2,1,0:T(8,128)(2,1)} %bitcast.116), calls=%async_computation | async-start | bytes 4194304 | tf_op jit(solution)/shard_map/all_to_all | solution.py:87
  130.5 81.3 %all-gather.2.cloned.1.call-start = ((), (), s32[]{:S(2)}) async-start(), calls=%async_computation.4 | async-start | bytes 1081344 | tf_op jit(solution)/shard_map/all_gather | solution.py:70
  217.3 6.5 %copy-start.2 = (bf16[256,1024]{1,0:T(8,128)(2,1)S(1)}, bf16[256,1024]{1,0:T(8,128)(2,1)}, u32[]{:S(2)}) copy-start(bf16[256,1024]{1,0:T(8,128)(2,1)} %param.16) | copy-start | bytes 1572868
  217.3 7.4 %copy-start.8 = (s32[1,8]{1,0:T(1,128)S(1)}, s32[1,8]{1,0:T(1,128)}, u32[]{:S(2)}) copy-start(s32[1,8]{1,0:T(1,128)} %param.13) | copy-start | bytes 100
  217.3 7.6 %copy-start.4 = (s32[256]{0:T(256)S(1)}, s32[256]{0:T(256)}, u32[]{:S(2)}) copy-start(s32[256]{0:T(256)} %param.14) | copy-start | bytes 3076
  217.3 99.4 %all-to-all-start.1 = ((bf16[8,4096,128]{2,1,0:T(8,128)(2,1)}), bf16[8,4096,128]{2,1,0:T(8,128)(2,1)}, u32[]{:S(2)}, u32[]{:S(2)}) async-start(bf16[8,4096,128]{2,1,0:T(8,128)(2,1)} %stack.2), calls=%async_computation.1 | async-start | bytes 16777216 | tf_op jit(solution)/shard_map/all_to_all | solution.py:11
  222.8 124.2 %reduce-scatter.2.cloned.1.call-start = ((), (), s32[]{:S(2)}) async-start(), calls=%async_computation.5 | async-start | bytes 147456 | tf_op jit(solution)/shard_map/reduce_scatter | solution.py:81
  327.0 13.3 %copy-start.3 = (f32[4096]{0:T(1024)S(1)}, f32[4096]{0:T(1024)}, u32[]{:S(2)}) copy-start(f32[4096]{0:T(1024)} %param.19) | copy-start | bytes 49156
  327.0 13.3 %copy-start.7 = (f32[1024]{0:T(1024)S(1)}, f32[1024]{0:T(1024)}, u32[]{:S(2)}) copy-start(f32[1024]{0:T(1024)} %param.21) | copy-start | bytes 12292
  347.1 1.6 copy-start.6
  348.3 7.5 %copy-start.5 = (f32[256]{0:T(256)}, f32[256]{0:T(256)S(1)}, u32[]{:S(2)}) copy-start(f32[256]{0:T(256)S(1)} %broadcast_multiply_fusion) | copy-start | bytes 3076
Sparse Core Ops, SparseCore 0:
  133.9 77.8 all-gather.1
Sparse Core Ops, SparseCore 1:
  226.4 29.6 reduce-scatter.1
